TPU v7x, 256 devices: a whole 4x4x8 slice. The times are simulated.
256 devices in a mesh: dp: 128 (over x, y_lo, z, core), section: 2 (over y_hi).
Axes of the slice: x: 4, y: 4 (y_hi: 2, y_lo: 2; y = y_hi * 2 + y_lo), z: 8, core: 2. Of those that a mesh axis runs over, the one named last changes fastest.
Arguments:
- replay_rows: bfloat16 [65536, 4, 4, 128], P('dp'), may hold values from -6 to 6
- qvalues: bfloat16 [65536, 18], P('dp'), may hold values from -5 to 129
- target_logits: bfloat16 [65536, 18], P('dp'), may hold values from -8 to 258
- replay_owner: int32 [32768], P(('dp', 'section')), may hold values from 0 to 127, as said below
- replay_slot: int32 [32768], P(('dp', 'section')), may hold values from 0 to 511
- sample_actions: int32 [32768, 20], P(('dp', 'section')), may hold values from 0 to 17
- weights: bfloat16 [2, 147456], replicated, may hold values from -0.1875 to 0.1875
- head: bfloat16 [128, 18], replicated, may hold values from -0.5 to 0.5
- master: float32 [2, 147456], P('section', 'dp'), may hold values from -0.0012 to 0.0012
- moment_first: float32 [2, 147456], P('section', 'dp'), may hold values from -0.0021 to 0.0021
- moment_second: float32 [2, 147456], P('section', 'dp'), may hold values from 9.9e-14 to 1.01e-06
Outputs:
- adam_step: float32 [2, 147456], P('section', 'dp')
- new_weights: bfloat16 [2, 147456], replicated
Inputs may be any that keep to these rules, and one draw needn't show every extreme that they name: `replay_owner`: among the 128 rows of one learner device no shard is named more than 2 times; in every draw one shard is named exactly 2 times by every learner device.
All inputs are finite; a program needn't handle non-finite values.
Results may differ from a plain program's by a relative error of at most 0.013.
Values may be sent and summed in bfloat16 or wider, within the bound.
No kernel may reach another device: no remote copies, remote signals or barrier semaphores. Data moves between devices by JAX's collectives and lax.ppermute only.
A program may use at most 192 MiB of HBM per device.

v0:
```python
import jax
import jax.numpy as jnp
from jax import lax
from jax.sharding import PartitionSpec as P

constant_entropy_scale = 0.5
trust_weight = 0.5
beta_first = 0.9
beta_second = 0.999
epsilon = 1e-08
learn_rate = 0.0001


def tap_stack(field):
    grid_side = field.shape[1]
    padded_rows = jnp.pad(field, ((0, 0), (1, 1), (1, 1), (0, 0)))
    return jnp.concatenate(
        [
            padded_rows[:, shift_row : shift_row + grid_side, shift_col : shift_col + grid_side, :]
            for shift_row in range(3)
            for shift_col in range(3)
        ],
        axis=-1,
    )


def layer_grads(
    features,
    move_return_estimates,
    reference_policy_entries,
    actions,
    row_scale,
    w_first,
    second_weight,
    head,
):
    row_count, grid_side, _, channels = features.shape
    positions = row_count * grid_side * grid_side
    taps_first = tap_stack(features).reshape(positions, 9 * channels)
    hidden = jax.nn.relu(jnp.dot(taps_first, w_first, preferred_element_type=jnp.float32)).astype(
        jnp.bfloat16
    )
    taps_second = tap_stack(hidden.reshape(features.shape)).reshape(positions, 9 * channels)
    summed = features.reshape(positions, channels).astype(jnp.float32) + jnp.dot(
        taps_second, second_weight, preferred_element_type=jnp.float32
    )
    block_out = jax.nn.relu(summed).astype(jnp.bfloat16)
    averaged_embedding = jnp.mean(
        block_out.astype(jnp.float32).reshape(row_count, grid_side * grid_side, channels), axis=1
    ).astype(jnp.bfloat16)
    logits = reference_policy_entries.astype(jnp.float32) + jnp.dot(
        averaged_embedding, head, preferred_element_type=jnp.float32
    )
    policy = jax.nn.softmax(logits, axis=-1)
    prior = jax.nn.softmax(reference_policy_entries.astype(jnp.float32), axis=-1)
    selected_moves = (actions[:, :, None] == jnp.arange(head.shape[1])[None, None, :]).astype(
        jnp.float32
    )
    move_logit_matrix = (
        jnp.einsum("vlu,vu->vl", selected_moves, move_return_estimates.astype(jnp.float32))
        / constant_entropy_scale
    )
    sample_weight = jax.nn.softmax(move_logit_matrix, axis=-1)
    logit_grad = (
        (1.0 + trust_weight) * policy
        - jnp.einsum("nk,nka->na", sample_weight, selected_moves)
        - trust_weight * prior
    ) * row_scale[:, None]
    pooled_grad = jnp.dot(logit_grad, head.astype(jnp.float32).T, precision=lax.Precision.HIGHEST)
    spread = jnp.broadcast_to(
        (pooled_grad / (grid_side * grid_side))[:, None, :],
        (row_count, grid_side * grid_side, channels),
    ).reshape(positions, channels)
    out_grad = jnp.where(block_out > 0, spread, 0.0).astype(jnp.bfloat16)
    grad_second = lax.dot_general(
        taps_second, out_grad, (((0,), (0,)), ((), ())), preferred_element_type=jnp.float32
    )
    flipped = (
        second_weight.reshape(9, channels, channels)[::-1]
        .transpose(0, 2, 1)
        .reshape(9 * channels, channels)
    )
    taps_back = tap_stack(out_grad.reshape(features.shape)).reshape(positions, 9 * channels)
    hidden_grad = jnp.where(
        hidden > 0, jnp.dot(taps_back, flipped, preferred_element_type=jnp.float32), 0.0
    ).astype(jnp.bfloat16)
    grad_first = lax.dot_general(
        taps_first, hidden_grad, (((0,), (0,)), ((), ())), preferred_element_type=jnp.float32
    )
    return (grad_first, grad_second)


def per_device(
    replay_rows,
    qvalues,
    target_logits,
    replay_owner,
    replay_slot,
    sample_actions,
    weights,
    head,
    master,
    moment_first,
    moment_second,
):
    rows_dev = replay_owner.shape[0]
    owners = lax.axis_size("dp")
    capacity = 2 * rows_dev // owners
    learn_rows = rows_dev * owners * lax.axis_size("section")
    channels = replay_rows.shape[3]
    w_first = weights[0].reshape(9 * channels, channels)
    second_weight = weights[1].reshape(9 * channels, channels)
    row_order = jnp.arange(rows_dev, dtype=jnp.int32)
    earlier = (replay_owner[None, :] == replay_owner[:, None]) & (
        row_order[None, :] < row_order[:, None]
    )
    rank_within = jnp.sum(earlier.astype(jnp.int32), axis=1)
    slot_index = replay_owner * capacity + rank_within
    matches = slot_index[None, :] == jnp.arange(owners * capacity, dtype=jnp.int32)[:, None]
    occupied_entries = jnp.any(matches, axis=1)
    source = jnp.sum(jnp.where(matches, row_order[None, :], 0), axis=1)
    request = jnp.where(occupied_entries, jnp.take(replay_slot, source), -1).reshape(
        owners, capacity
    )
    row_index = jnp.maximum(
        lax.all_to_all(request, "dp", split_axis=0, concat_axis=0, tiled=True), 0
    )
    feature_slots = lax.all_to_all(
        jnp.take(replay_rows, row_index, axis=0), "dp", split_axis=0, concat_axis=0, tiled=True
    )
    qvalue_slots = lax.all_to_all(
        jnp.take(qvalues, row_index, axis=0), "dp", split_axis=0, concat_axis=0, tiled=True
    )
    prior_slots = lax.all_to_all(
        jnp.take(target_logits, row_index, axis=0), "dp", split_axis=0, concat_axis=0, tiled=True
    )
    features = jnp.take(
        feature_slots.reshape((owners * capacity,) + feature_slots.shape[2:]), slot_index, axis=0
    )
    move_return_estimates = jnp.take(
        qvalue_slots.reshape(owners * capacity, -1), slot_index, axis=0
    )
    reference_policy_entries = jnp.take(
        prior_slots.reshape(owners * capacity, -1), slot_index, axis=0
    )
    row_scale = jnp.full((rows_dev,), 1.0 / learn_rows, jnp.float32)
    grad_first, grad_second = layer_grads(
        features,
        move_return_estimates,
        reference_policy_entries,
        sample_actions,
        row_scale,
        w_first,
        second_weight,
        head,
    )
    loss_derivative = jnp.stack([grad_first.reshape(-1), grad_second.reshape(-1)])
    piece_len = loss_derivative.shape[1] // owners
    regrouped = (
        loss_derivative.reshape(2, owners, piece_len)
        .transpose(1, 0, 2)
        .reshape(2 * owners, piece_len)
    )
    owned_grad = lax.psum_scatter(regrouped, ("dp", "section"), scatter_dimension=0, tiled=True)
    first = beta_first * moment_first + (1.0 - beta_first) * owned_grad
    second = beta_second * moment_second + (1.0 - beta_second) * owned_grad * owned_grad
    adam_step = first / (jnp.sqrt(second) + epsilon)
    new_piece = (master - learn_rate * adam_step).astype(jnp.bfloat16)
    collected = lax.all_gather(new_piece, ("dp", "section"), axis=0, tiled=True)
    new_weights = (
        collected.reshape(owners, 2, piece_len).transpose(1, 0, 2).reshape(2, owners * piece_len)
    )
    return (adam_step, new_weights)


def solution(mesh):
    placed = (
        P("dp", None, None, None),
        P("dp", None),
        P("dp", None),
        P(("dp", "section")),
        P(("dp", "section")),
        P(("dp", "section"), None),
        P(),
        P(),
        P("section", "dp"),
        P("section", "dp"),
        P("section", "dp"),
    )
    return jax.shard_map(
        per_device, mesh=mesh, in_specs=placed, out_specs=(P("section", "dp"), P()), check_vma=False
    )
```

profile of v0, /device:TPU:0, one launch (start us, length us, event | category | flops | bytes accessed | tf_op | source)
XLA Modules:
  0.0 1061.6 jit_solution(8042441142103392493)
XLA Ops:
  9.4 1.9 gather_fusion
  12.1 12.5 %all-to-all-start = ((s32[128,1,2]{2,1,0:T(1,128)}), s32[128,1,2]{2,1,0:T(1,128)S(1)}, u32[]{:S(2)}, u32[]{:S(2)}) async-start(s32[128,1,2]{2,1,0:T(1,128)} %bitcast.3), calls=%async_computation | async-start | bytes 131072 | tf_op jit(solution)/shard_map/all_to_all | solution.py:126
  26.4 8.6 all-to-all-done
  37.9 6.2 all-to-all-start.3
  45.7 8.9 all-to-all-done.3
  54.6 6.1 all-to-all-start.2
  62.3 8.9 all-to-all-done.2
  71.1 6.2 all-to-all-start.1
  77.8 8.4 slice_reduce_fusion
  87.7 1.8 copy.42
  91.5 14.9 %all-to-all-done.1 = bf16[128,2,4,4,128]{4,3,2,1,0:T(4,128)(2,1)S(1)} async-done(((bf16[128,2,4,4,128]{4,3,2,1,0:T(4,128)(2,1)}), bf16[128,2,4,4,128]{4,3,2,1,0:T(4,128)(2,1)S(1)}, u32[]{:S(2)}, u32[]{:S(2)}) %all-to-all-start.1) | async-done | bytes 1048608 | tf_op jit(solution)/shard_map/all_to_all | solution.py:128
  107.4 2.3 gather_fusion.2
  120.3 8.5 reshape.203
  128.9 3.7 fusion.2
  135.5 1.9 convert_reduce_fusion
  138.1 2.3 fusion.53
  141.5 1.8 pad_slice_fusion
  144.5 2.2 copy-done.7
  146.7 8.8 fusion.5
  157.7 1.9 reshape.212
  159.6 258.0 %all-reduce.6.cloned.1.call-done = f32[256,1152]{1,0:T(8,128)} async-done(((f32[256,1152]{1,0:T(8,128)}), f32[256,1152]{1,0:T(8,128)}) %all-reduce.6.cloned.1.call-update) | async-done | bytes 1179664
  419.0 628.6 %all-gather = bf16[256,1,1152]{2,1,0:T(2,128)(2,1)S(1)} all-gather(bf16[1,1,1152]{2,1,0:T(2,128)(2,1)S(1)} %get-tuple-element.6), channel_id=1, replica_groups=mesh['dp'=128,'section'=2] {'dp','section'}, dimensions={0}, use_global_device_ids=true | all-gather | bytes 592128 | tf_op jit(solution)/shard_map/all_gather | solution.py:169
  1047.6 4.4 reduce.6
  1052.0 2.6 reshape.213
  (106 shorter events, 35.6 us)
Async XLA Ops:
  7.2 37.0 %copy-start = (bf16[512,4,4,128]{3,2,1,0:T(4,128)(2,1)S(1)}, bf16[512,4,4,128]{3,2,1,0:T(4,128)(2,1)}, u32[]{:S(2)}) copy-start(bf16[512,4,4,128]{3,2,1,0:T(4,128)(2,1)} %param.15) | copy-start | bytes 6291460
  12.1 22.9 %all-to-all-start = ((s32[128,1,2]{2,1,0:T(1,128)}), s32[128,1,2]{2,1,0:T(1,128)S(1)}, u32[]{:S(2)}, u32[]{:S(2)}) async-start(s32[128,1,2]{2,1,0:T(1,128)} %bitcast.3), calls=%async_computation | async-start | bytes 131072 | tf_op jit(solution)/shard_map/all_to_all | solution.py:126
  37.9 16.6 %all-to-all-start.3 = ((bf16[128,2,18]{2,1,0:T(2,128)(2,1)}), bf16[128,2,18]{2,1,0:T(2,128)(2,1)S(1)}, u32[]{:S(2)}, u32[]{:S(2)}) async-start(bf16[128,2,18]{2,1,0:T(2,128)(2,1)} %get-tuple-element.29), calls=%async_computation.3 | async-start | bytes 131072 | tf_op jit(solution)/shard_map/all_to_all | solution.py:131
  44.1 47.2 %copy-start.8 = (s32[128,20]{0,1:T(8,128)S(1)}, s32[128,20]{0,1:T(8,128)}, u32[]{:S(2)}) copy-start(s32[128,20]{0,1:T(8,128)} %param.20) | copy-start | bytes 30724
  54.6 16.6 %all-to-all-start.2 = ((bf16[128,2,18]{2,1,0:T(2,128)(2,1)}), bf16[128,2,18]{2,1,0:T(2,128)(2,1)S(1)}, u32[]{:S(2)}, u32[]{:S(2)}) async-start(bf16[128,2,18]{2,1,0:T(2,128)(2,1)} %get-tuple-element.28), calls=%async_computation.2 | async-start | bytes 131072 | tf_op jit(solution)/shard_map/all_to_all | solution.py:134
  71.1 35.3 %all-to-all-start.1 = ((bf16[128,2,4,4,128]{4,3,2,1,0:T(4,128)(2,1)}), bf16[128,2,4,4,128]{4,3,2,1,0:T(4,128)(2,1)S(1)}, u32[]{:S(2)}, u32[]{:S(2)}) async-start(bf16[128,2,4,4,128]{4,3,2,1,0:T(4,128)(2,1)} %broadcast_select_fusion), calls=%async_computation.1 | async-start | bytes 2097152 | tf_op jit(solution)/shard_map/all_to_all | solution.py:128
  77.3 340.2 %all-reduce.6.cloned.1.call-start = ((), (), s32[]{:S(2)}) async-start(), calls=%async_computation.4 | async-start | bytes 2359296
  86.2 0.7 copy-start.3
  106.4 1.0 copy-start.1
  120.3 8.5 copy-start.5
  132.6 2.4 copy-start.2
  134.3 1.2 copy-start.4
  135.5 1.9 copy-start.9
  143.3 3.4 copy-start.6
  144.5 2.2 copy-start.7
  155.5 262.1 %copy-start.10 = (f32[1,1152]{1,0:T(1,128)S(1)}, f32[1,1152]{1,0:T(1,128)}, u32[]{:S(2)}) copy-start(f32[1,1152]{1,0:T(1,128)} %param.23) | copy-start | bytes 13828
  155.5 262.1 %copy-start.11 = (f32[1,1152]{1,0:T(1,128)S(1)}, f32[1,1152]{1,0:T(1,128)}, u32[]{:S(2)}) copy-start(f32[1,1152]{1,0:T(1,128)} %param.25) | copy-start | bytes 13828
  155.5 262.1 %copy-start.12 = (f32[1,1152]{1,0:T(1,128)S(1)}, f32[1,1152]{1,0:T(1,128)}, u32[]{:S(2)}) copy-start(f32[1,1152]{1,0:T(1,128)} %param.24) | copy-start | bytes 13828
Sparse Core Ops, SparseCore 0:
  159.7 257.8 all-reduce.5
where the time goes:
time: 1070 us; the launch traced here: 1060 us
  blocking collectives  629 us (59%)
  waiting for transfers between devices  299 us (28%)
  local copies, waits for them, and re-layouts  57.9 us (5%)
  starting transfers between devices  31 us (3%)
  matrix products  17.1 us (2%)
  between operations  14.8 us (1%)
  other arithmetic  12.8 us (1%)
    all_gather x1, blocking collectives, per_device(): collected = lax.all_gather(new_piece, ('dp', 'section'), axis=0, tiled=True)  629 us
    unnamed x2, waiting for transfers between devices  258 us
  transfers between devices with their start and end apart: 5, of which 5 were waited for; matrix products, arithmetic and copies ran while one was open for 2% of the time, Pallas kernels for 0%

commit v1 on v0

--- a/solution.py
+++ b/solution.py
@@ -166,7 +166,10 @@
     second = beta_second * moment_second + (1.0 - beta_second) * owned_grad * owned_grad
     adam_step = first / (jnp.sqrt(second) + epsilon)
     new_piece = (master - learn_rate * adam_step).astype(jnp.bfloat16)
-    collected = lax.all_gather(new_piece, ("dp", "section"), axis=0, tiled=True)
+    z = tuple((new_piece for _ in range(lax.axis_size(("dp", "section")))))
+    t1 = jnp.stack(z, 0)
+    raw_out = lax.all_to_all(t1, ("dp", "section"), 0, 0)
+    collected = jnp.concatenate(raw_out, 0)
     new_weights = (
         collected.reshape(owners, 2, piece_len).transpose(1, 0, 2).reshape(2, owners * piece_len)
     )

time: 1070 us -> 491 us (0.46)
  the two profiles are of different devices: /device:TPU:0 before, /device:TPU:1 now
where the time goes in v1:
time: 491 us; the launch traced here: 482 us
  waiting for transfers between devices  298 us (61%)
  local copies, waits for them, and re-layouts  66 us (13%)
  blocking collectives  34.4 us (7%)
  starting transfers between devices  32.2 us (7%)
  other arithmetic  19 us (4%)
  matrix products  17.2 us (4%)
  between operations  15 us (3%)
    unnamed x2, waiting for transfers between devices  254 us
    all_to_all x1, blocking collectives, per_device(): raw_out = lax.all_to_all(t1, ('dp', 'section'), 0, 0)  34.4 us
    unnamed x54, local copies, waits for them, and re-layouts  22.1 us
    all_to_all x1, waiting for transfers between devices, per_device(): lax.all_to_all(jnp.take(replay_rows, row_index, axis=0), 'dp', split_axis...  16.6 us
    all_to_all x1, starting transfers between devices, per_device(): lax.all_to_all(request, 'dp', split_axis=0, concat_axis=0, tiled=True)  14.8 us
  transfers between devices with their start and end apart: 5, of which 5 were waited for; matrix products, arithmetic and copies ran while one was open for 4% of the time, Pallas kernels for 0%

profile of v1, /device:TPU:1, one launch (start us, length us, event | category | flops | bytes accessed | tf_op | source)
XLA Modules:
  0.0 481.7 jit_solution(2882919465159461653)
XLA Ops:
  12.1 14.8 %all-to-all-start = ((s32[128,1,2]{2,1,0:T(1,128)}), s32[128,1,2]{2,1,0:T(1,128)S(1)}, u32[]{:S(2)}, u32[]{:S(2)}) async-start(s32[128,1,2]{2,1,0:T(1,128)} %bitcast.3), calls=%async_computation | async-start | bytes 131072 | tf_op jit(solution)/shard_map/all_to_all | solution.py:126
  28.7 8.9 %all-to-all-done = s32[128,1,2]{2,1,0:T(1,128)S(1)} async-done(((s32[128,1,2]{2,1,0:T(1,128)}), s32[128,1,2]{2,1,0:T(1,128)S(1)}, u32[]{:S(2)}, u32[]{:S(2)}) %all-to-all-start) | async-done | bytes 1056 | tf_op jit(solution)/shard_map/all_to_all | solution.py:126
  40.5 5.8 %all-to-all-start.3 = ((bf16[128,2,18]{2,1,0:T(2,128)(2,1)}), bf16[128,2,18]{2,1,0:T(2,128)(2,1)S(1)}, u32[]{:S(2)}, u32[]{:S(2)}) async-start(bf16[128,2,18]{2,1,0:T(2,128)(2,1)} %get-tuple-element.29), calls=%async_computation.3 | async-start | bytes 131072 | tf_op jit(solution)/shard_map/all_to_all | solution.py:131
  47.9 9.3 %all-to-all-done.3 = bf16[128,2,18]{2,1,0:T(2,128)(2,1)S(1)} async-done(((bf16[128,2,18]{2,1,0:T(2,128)(2,1)}), bf16[128,2,18]{2,1,0:T(2,128)(2,1)S(1)}, u32[]{:S(2)}, u32[]{:S(2)}) %all-to-all-start.3) | async-done | bytes 9248 | tf_op jit(solution)/shard_map/all_to_all | solution.py:131
  57.2 5.8 %all-to-all-start.2 = ((bf16[128,2,18]{2,1,0:T(2,128)(2,1)}), bf16[128,2,18]{2,1,0:T(2,128)(2,1)S(1)}, u32[]{:S(2)}, u32[]{:S(2)}) async-start(bf16[128,2,18]{2,1,0:T(2,128)(2,1)} %get-tuple-element.28), calls=%async_computation.2 | async-start | bytes 131072 | tf_op jit(solution)/shard_map/all_to_all | solution.py:134
  64.5 9.3 %all-to-all-done.2 = bf16[128,2,18]{2,1,0:T(2,128)(2,1)S(1)} async-done(((bf16[128,2,18]{2,1,0:T(2,128)(2,1)}), bf16[128,2,18]{2,1,0:T(2,128)(2,1)S(1)}, u32[]{:S(2)}, u32[]{:S(2)}) %all-to-all-start.2) | async-done | bytes 9248 | tf_op jit(solution)/shard_map/all_to_all | solution.py:134
  73.7 5.8 %all-to-all-start.1 = ((bf16[128,2,4,4,128]{4,3,2,1,0:T(4,128)(2,1)}), bf16[128,2,4,4,128]{4,3,2,1,0:T(4,128)(2,1)S(1)}, u32[]{:S(2)}, u32[]{:S(2)}) async-start(bf16[128,2,4,4,128]{4,3,2,1,0:T(4,128)(2,1)} %broadcast_select_fusion), calls=%async_computation.1 | async-start | bytes 2097152 | tf_op jit(solution)/shard_map/all_to_all | solution.py:128
  80.0 8.1 %slice_reduce_fusion = (bf16[147456]{0:T(1024)(128)(2,1)S(1)}, bf16[147456]{0:T(1024)(128)(2,1)}) fusion(bf16[2,147456]{1,0:T(2,128)(2,1)} %param.21), kind=kLoop, calls=%fused_computation.46 | loop fusion | bytes 1179648 | tf_op jit(solution)/shard_map/slice | solution.py:112
  93.4 16.6 %all-to-all-done.1 = bf16[128,2,4,4,128]{4,3,2,1,0:T(4,128)(2,1)S(1)} async-done(((bf16[128,2,4,4,128]{4,3,2,1,0:T(4,128)(2,1)}), bf16[128,2,4,4,128]{4,3,2,1,0:T(4,128)(2,1)S(1)}, u32[]{:S(2)}, u32[]{:S(2)}) %all-to-all-start.1) | async-done | bytes 1048608 | tf_op jit(solution)/shard_map/all_to_all | solution.py:128
  111.0 2.3 gather_fusion.2
  123.9 8.5 %reshape.203 = bf16[2048,1152]{1,0:T(8,128)(2,1)} reshape(bf16[128,4,4,1152]{3,2,1,0:T(4,128)(2,1)} %fusion.13) | data formatting | bytes 9437184 | tf_op jit(solution)/shard_map/reshape | solution.py:39
  132.5 3.7 fusion.2
  139.1 1.9 convert_reduce_fusion
  141.8 2.3 fusion.53
  148.1 2.2 copy-done.7
  150.3 8.8 %fusion.5 = f32[1152,128]{1,0:T(8,128)} fusion(bf16[2048,1152]{1,0:T(8,128)(2,1)} %reshape.203, bf16[2048,1152]{1,0:T(8,128)(2,1)} %copy-done.7, bf16[1152,128]{1,0:T(8,128)(2,1)S(1)} %bitcast.101, bf16[2048,128]{1,0:T(8,128)(2,1)} %copy-done.2), kind=kOutput, calls=%fused_computation.45 | convolution fusion | flops 1208745984 | bytes 10846208 | tf_op jit(solution)/shard_map/dot_general | solution.py:87
  159.1 2.0 stack.8
  165.1 253.9 %all-reduce.6.cloned.1.call-done = f32[256,1152]{1,0:T(8,128)} async-done(((f32[256,1152]{1,0:T(8,128)}), f32[256,1152]{1,0:T(8,128)}) %all-reduce.6.cloned.1.call-update) | async-done | bytes 1179664
  421.6 5.1 %reduce.13 = bf16[256,1152]{1,0:T(8,128)(2,1)} reduce(bf16[256,1,1152]{2,1,0:T(2,128)(2,1)S(1)} %stack.11, bf16[]{:T(256)} %broadcast.181), dimensions={1}, to_apply=%stack.11.reduce_sub_computation | reduce | bytes 1179650 | tf_op jit(solution)/shard_map/stack | solution.py:170
  426.7 2.2 reshape.302
  428.9 34.4 %all_to_all.26 = bf16[256,2,576]{2,1,0:T(2,128)(2,1)} all-to-all(bf16[256,2,576]{2,1,0:T(2,128)(2,1)S(1)} %reshape.302), channel_id=1, replica_groups=mesh['dp'=128,'section'=2] {'dp','section'}, dimensions={0} | all-to-all | bytes 1179648 | tf_op jit(solution)/shard_map/all_to_all | solution.py:171
  463.3 4.2 reshape.303
  467.5 4.4 reduce.7
  471.9 2.6 reshape_reshape.3
  (111 shorter events, 44.0 us)
Async XLA Ops:
  7.2 39.1 %copy-start = (bf16[512,4,4,128]{3,2,1,0:T(4,128)(2,1)S(1)}, bf16[512,4,4,128]{3,2,1,0:T(4,128)(2,1)}, u32[]{:S(2)}) copy-start(bf16[512,4,4,128]{3,2,1,0:T(4,128)(2,1)} %param.15) | copy-start | bytes 6291460
  12.1 25.4 %all-to-all-start = ((s32[128,1,2]{2,1,0:T(1,128)}), s32[128,1,2]{2,1,0:T(1,128)S(1)}, u32[]{:S(2)}, u32[]{:S(2)}) async-start(s32[128,1,2]{2,1,0:T(1,128)} %bitcast.3), calls=%async_computation | async-start | bytes 131072 | tf_op jit(solution)/shard_map/all_to_all | solution.py:126
  40.5 16.6 %all-to-all-start.3 = ((bf16[128,2,18]{2,1,0:T(2,128)(2,1)}), bf16[128,2,18]{2,1,0:T(2,128)(2,1)S(1)}, u32[]{:S(2)}, u32[]{:S(2)}) async-start(bf16[128,2,18]{2,1,0:T(2,128)(2,1)} %get-tuple-element.29), calls=%async_computation.3 | async-start | bytes 131072 | tf_op jit(solution)/shard_map/all_to_all | solution.py:131
  46.3 46.9 %copy-start.8 = (s32[128,20]{0,1:T(8,128)S(1)}, s32[128,20]{0,1:T(8,128)}, u32[]{:S(2)}) copy-start(s32[128,20]{0,1:T(8,128)} %param.20) | copy-start | bytes 30724
  57.2 16.6 %all-to-all-start.2 = ((bf16[128,2,18]{2,1,0:T(2,128)(2,1)}), bf16[128,2,18]{2,1,0:T(2,128)(2,1)S(1)}, u32[]{:S(2)}, u32[]{:S(2)}) async-start(bf16[128,2,18]{2,1,0:T(2,128)(2,1)} %get-tuple-element.28), calls=%async_computation.2 | async-start | bytes 131072 | tf_op jit(solution)/shard_map/all_to_all | solution.py:134
  73.7 36.3 %all-to-all-start.1 = ((bf16[128,2,4,4,128]{4,3,2,1,0:T(4,128)(2,1)}), bf16[128,2,4,4,128]{4,3,2,1,0:T(4,128)(2,1)S(1)}, u32[]{:S(2)}, u32[]{:S(2)}) async-start(bf16[128,2,4,4,128]{4,3,2,1,0:T(4,128)(2,1)} %broadcast_select_fusion), calls=%async_computation.1 | async-start | bytes 2097152 | tf_op jit(solution)/shard_map/all_to_all | solution.py:128
  79.5 339.5 %all-reduce.6.cloned.1.call-start = ((), (), s32[]{:S(2)}) async-start(), calls=%async_computation.5 | async-start | bytes 2359296
  88.1 0.7 copy-start.3
  110.0 1.0 copy-start.1
  123.9 8.5 %copy-start.5 = (bf16[147456]{0:T(1024)(128)(2,1)S(1)}, bf16[147456]{0:T(1024)(128)(2,1)}, u32[]{:S(2)}) copy-start(bf16[147456]{0:T(1024)(128)(2,1)} %get-tuple-element.5) | copy-start | bytes 884740
  136.2 2.4 copy-start.2
  137.9 1.2 copy-start.4
  139.1 2.0 copy-start.9
  146.9 3.4 copy-start.6
  148.1 2.2 copy-start.7
  159.1 259.9 %copy-start.10 = (f32[1,1152]{1,0:T(1,128)S(1)}, f32[1,1152]{1,0:T(1,128)}, u32[]{:S(2)}) copy-start(f32[1,1152]{1,0:T(1,128)} %param.23) | copy-start | bytes 13828
  159.1 259.9 %copy-start.11 = (f32[1,1152]{1,0:T(1,128)S(1)}, f32[1,1152]{1,0:T(1,128)}, u32[]{:S(2)}) copy-start(f32[1,1152]{1,0:T(1,128)} %param.25) | copy-start | bytes 13828
  159.1 259.9 %copy-start.12 = (f32[1,1152]{1,0:T(1,128)S(1)}, f32[1,1152]{1,0:T(1,128)}, u32[]{:S(2)}) copy-start(f32[1,1152]{1,0:T(1,128)} %param.24) | copy-start | bytes 13828
Sparse Core Ops, SparseCore 0:
  165.2 253.7 all-reduce.5
